TPU v7x, 256 devices: a whole 4x4x8 slice. The times are simulated.
256 devices in a mesh: exp: 64 (over y, z, core), grp: 4 (over x).
Axes of the slice: x: 4, y: 4, z: 8, core: 2. Of those that a mesh axis runs over, the one named last changes fastest.
Arguments:
- tiles: bfloat16 [1024, 256, 256], P(('exp', 'grp')), may hold values from -6 to 6
- tile_exposure: int32 [1024], P(('exp', 'grp')), may hold values from 0 to 511, as said below
- tile_patch: int32 [1024, 4], P(('exp', 'grp')), may hold values from 0 to 63, all different within a row; in each aligned block of 4 rows (0 to 3, 4 to 7, ...) at most 2 rows name the same one
- tile_offset: int32 [1024, 4, 2], P(('exp', 'grp')), may hold values from 0 to 256
- coeffs: bfloat16 [512, 10], P(('exp', 'grp')), may hold values from -2 to 2
- inv_var: bfloat16 [512], P(('exp', 'grp')), may hold values from 0.25 to 4
- vert_taps: bfloat16 [10, 41], replicated, may hold values from -1 to 1
- horiz_taps: bfloat16 [10, 41], replicated, may hold values from -1 to 1
Outputs:
- coadd: float32 [64, 512, 512], P('exp', 'grp')
Inputs may be any that keep to these rules, and one draw needn't show every extreme that they name: `tile_exposure`: each exposure is named by exactly 1024 / 512 tiles. `tile_patch`: the entries of a row differ; among the rows of one device no patch is named by more than 2 rows. `tile_offset`: each tile lies wholly inside each patch listed for it.
All inputs are finite; a program needn't handle non-finite values.
Results may differ from a plain program's by a relative error of at most 0.0041.
Values may be sent and summed in bfloat16 or wider, within the bound.
No kernel may reach another device: no remote copies, remote signals or barrier semaphores. Data moves between devices by JAX's collectives and lax.ppermute only.
A program may use at most 128 MiB of HBM per device.

v0:
```python
import math
import jax
import jax.numpy as jnp
from jax import lax
from jax.sharding import PartitionSpec as P

PS = 512


def band_matrix(filters, tile_side):
    terms, kernel_width = filters.shape
    half_width = (kernel_width - 1) // 2
    padding = tile_side - 1 - half_width
    padded = jnp.concatenate(
        [
            jnp.zeros((terms, padding), jnp.float32),
            filters.astype(jnp.float32),
            jnp.zeros((terms, padding + 1), jnp.float32),
        ],
        axis=1,
    )
    tiled = jnp.tile(padded, (1, tile_side + 1))[:, : tile_side * (2 * tile_side + 1)]
    window = tiled.reshape(terms, tile_side, 2 * tile_side + 1)[:, :, :tile_side]
    return window[:, ::-1, :].astype(jnp.bfloat16)


def coverage_rows(tags, row_count, tile_side, patch_side):
    weights = tags[:, 0].astype(jnp.float32)
    row_off = tags[:, 1].astype(jnp.int32)
    col_off = tags[:, 2].astype(jnp.int32)
    row_index = jnp.arange(row_count, dtype=jnp.int32)
    col_index = jnp.arange(patch_side, dtype=jnp.int32)
    row_mask = (
        (row_index[None, :] >= row_off[:, None])
        & (row_index[None, :] < row_off[:, None] + tile_side)
    ).astype(jnp.float32) * weights[:, None]
    col_mask = (
        (col_index[None, :] >= col_off[:, None])
        & (col_index[None, :] < col_off[:, None] + tile_side)
    ).astype(jnp.float32)
    return jnp.einsum("sy,sx->yx", row_mask, col_mask, precision=lax.Precision.HIGHEST)


def per_device(
    tiles, tile_exposure, tile_patch, tile_offset, coeffs, inv_var, vert_taps, horiz_taps
):
    n_owners = lax.axis_size("exp")
    tile_count = tiles.shape[0]
    tile_side = tiles.shape[1]
    listed = tile_patch.shape[1]
    entries = tile_count * listed
    capacity = max(2, (entries + n_owners - 1) // n_owners)
    slot_total = n_owners * capacity
    coef_all, weight_all = (
        lax.all_gather(coeffs, ("exp", "grp"), axis=0, tiled=True),
        lax.all_gather(inv_var, ("exp", "grp"), axis=0, tiled=True),
    )
    exposures = coef_all.shape[0]
    picker = (tile_exposure[:, None] == jnp.arange(exposures, dtype=jnp.int32)[None, :]).astype(
        jnp.bfloat16
    )
    coef_tile = jnp.dot(picker, coef_all, preferred_element_type=jnp.float32)
    weight_tile = jnp.dot(picker, weight_all[:, None], preferred_element_type=jnp.float32)[:, 0]
    vband = band_matrix(vert_taps, tile_side)
    hband = band_matrix(horiz_taps, tile_side)

    def convolve_one(inputs):
        one_tile, coef_row, weight = inputs
        rows_pass = jnp.einsum("yk,bxk->ybx", one_tile, hband, preferred_element_type=jnp.float32)
        partial_value = (rows_pass * coef_row[None, :, None]).astype(jnp.bfloat16)
        smoothed = jnp.einsum(
            "byk,kbx->yx", vband, partial_value, preferred_element_type=jnp.float32
        )
        return (weight * smoothed).astype(jnp.bfloat16)

    weighted = lax.map(convolve_one, (tiles, coef_tile, weight_tile))
    owners = tile_patch.reshape(entries)
    onehot = (owners[:, None] == jnp.arange(n_owners, dtype=jnp.int32)[None, :]).astype(jnp.int32)
    before = jnp.cumsum(onehot, axis=0) - onehot
    rank = jnp.sum(before * onehot, axis=1)
    target = owners * capacity + rank
    offsets = tile_offset.reshape(entries, 2)
    entry_tiles = jnp.repeat(weighted, listed, axis=0)
    entry_tags = jnp.stack(
        [
            jnp.repeat(weight_tile, listed),
            offsets[:, 0].astype(jnp.float32),
            offsets[:, 1].astype(jnp.float32),
        ],
        axis=1,
    ).astype(jnp.bfloat16)
    send_tiles = (
        jnp.zeros((slot_total, tile_side, tile_side), jnp.bfloat16).at[target].set(entry_tiles)
    )
    send_tags = jnp.zeros((slot_total, 3), jnp.bfloat16).at[target].set(entry_tags)
    got_tiles, got_tags = (
        lax.all_to_all(send_tiles, "exp", split_axis=0, concat_axis=0, tiled=True),
        lax.all_to_all(send_tags, "exp", split_axis=0, concat_axis=0, tiled=True),
    )
    got_rows = got_tags[:, 1].astype(jnp.int32)
    got_cols = got_tags[:, 2].astype(jnp.int32)
    block_slots = math.gcd(slot_total, 32)
    block_count = slot_total // block_slots
    inner = jnp.arange(tile_side, dtype=jnp.int32)
    col_index = jnp.arange(PS, dtype=jnp.int32)

    def place_block(canvas, inputs):
        block_tiles, block_rows, block_cols = inputs
        shifter = (
            col_index[None, None, :] == block_cols[:, None, None] + inner[None, :, None]
        ).astype(jnp.bfloat16)
        shifted = jnp.einsum(
            "syk,skx->syx", block_tiles, shifter, preferred_element_type=jnp.float32
        )
        row_index = (block_rows[:, None] + inner[None, :]).reshape(-1)
        canvas = canvas.at[row_index].add(shifted.reshape(-1, PS))
        return (canvas, None)

    flux, _ = lax.scan(
        place_block,
        jnp.zeros((PS, PS), jnp.float32),
        (
            got_tiles.reshape(block_count, block_slots, tile_side, tile_side),
            got_rows.reshape(block_count, block_slots),
            got_cols.reshape(block_count, block_slots),
        ),
    )
    cover = coverage_rows(got_tags, PS, tile_side, PS)
    flux_band, cover_band = (
        lax.psum_scatter(flux, "grp", scatter_dimension=0, tiled=True),
        lax.psum_scatter(cover, "grp", scatter_dimension=0, tiled=True),
    )
    coadd = flux_band / jnp.maximum(cover_band, 1.0)
    return coadd[None]


def solution(mesh):
    in_specs = (
        P(("exp", "grp"), None, None),
        P(("exp", "grp")),
        P(("exp", "grp"), None),
        P(("exp", "grp"), None, None),
        P(("exp", "grp"), None),
        P(("exp", "grp")),
        P(),
        P(),
    )
    out_specs = P("exp", "grp", None)
    return jax.shard_map(
        per_device, mesh=mesh, in_specs=in_specs, out_specs=out_specs, check_vma=False
    )
```

profile of v0, /device:TPU:8, one launch (start us, length us, event | category | flops | bytes accessed | tf_op | source)
XLA Modules:
  0.0 925.7 jit_solution(5432011449631272837)
XLA Ops:
  6.5 0.8 eq.20
  7.3 0.7 broadcast_multiply_fusion
  8.1 0.2 select_reduce_fusion
  8.4 0.8 dynamic-update-slice
  9.2 78.6 %all-reduce = bf16[512]{0:T(512)(128)(2,1)S(1)} all-reduce(bf16[512]{0:T(512)(128)(2,1)S(1)} %dynamic-update-slice), channel_id=1, replica_groups=mesh['exp'=64,'grp'=4] {'exp','grp'}, use_global_device_ids=true, to_apply=%add | all-reduce | flops 512 | bytes 2048
  87.8 0.8 fusion.48
  88.8 0.7 copy.16
  89.6 0.1 copy.17
  89.7 1.2 scatter_custom_fusion.1
  90.9 8.2 all-to-all-start
  99.3 0.8 maximum_maximum_fusion.1
  100.1 0.2 tile.8
  100.3 0.3 pad.9
  100.5 1.6 copy.31
  102.1 2.1 slice.39
  104.2 8.3 reshape.146
  112.5 1.2 slice.40
  113.7 19.4 %rev.6 = bf16[10,256,256]{2,1,0:T(8,128)(2,1)} reverse(bf16[10,256,256]{2,1,0:T(8,128)(2,1)} %slice.40), dimensions={1} | reverse | bytes 2621440 | tf_op jit(solution)/shard_map/rev | solution.py:24
  133.1 0.2 tile.20
  133.2 0.3 pad.10
  133.5 1.6 copy.32
  135.1 2.1 slice.41
  137.2 8.3 reshape.147
  145.6 1.2 slice.42
  146.7 15.8 %rev.7 = bf16[10,256,256]{2,1,0:T(8,128)(2,1)S(1)} reverse(bf16[10,256,256]{2,1,0:T(8,128)(2,1)} %slice.42), dimensions={1} | reverse | bytes 2621440 | tf_op jit(solution)/shard_map/rev | solution.py:24
  162.5 89.8 %all-gather = bf16[256,2,10]{2,1,0:T(2,128)(2,1)S(1)} all-gather(bf16[1,2,10]{2,1,0:T(2,128)(2,1)S(1)} %bitcast.109), channel_id=1, replica_groups=mesh['exp'=64,'grp'=4] {'exp','grp'}, dimensions={0}, use_global_device_ids=true | all-gather | bytes 10280 | tf_op jit(solution)/shard_map/all_gather | solution.py:55
  252.3 0.2 fusion.39
  252.5 19.2 %while.22 = (s32[]{:T(128)}, bf16[4,256,256]{2,1,0:T(8,128)(2,1)}, f32[4]{0:T(128)S(1)}, bf16[4,256,256]{2,1,0:T(8,128)(2,1)}, bf16[10,256,256]{2,1,0:T(8,128)(2...) while((s32[]{:T(128)}, bf16[4,256,256]{2,1,0:T(8,128)(2,1)}, f32[4]{0:T(128)S(1)}, ...), condition=%wide.region_3.4_spmd, body=%wide.region_2.3_spmd.sunk | while | flops 672530432 | bytes 3409629 | solution.py:76
  252.5 0.7 dynamic_slice.54
  253.2 3.3 fusion.66
  256.5 0.1 copy.35
  256.6 0.7 constant_dynamic-update-slice_fusion.2
  257.3 0.7 dynamic_slice.54
  258.0 3.3 fusion.66
  261.4 0.1 copy.35
  261.5 0.7 constant_dynamic-update-slice_fusion.2
  262.1 0.7 dynamic_slice.54
  262.8 3.3 fusion.66
  266.2 0.1 copy.35
  266.3 0.7 constant_dynamic-update-slice_fusion.2
  266.9 0.7 dynamic_slice.54
  267.6 3.3 fusion.66
  271.0 0.1 copy.35
  271.1 0.7 constant_dynamic-update-slice_fusion.2
  271.7 1.2 broadcast_in_dim.30
  273.0 5.9 broadcast_in_dim.28
  278.9 5.3 scatter_fusion.1
  284.2 9.3 %all-to-all-start.1 = ((bf16[128,256,256]{2,1,0:T(8,128)(2,1)}), bf16[128,256,256]{2,1,0:T(8,128)(2,1)}, u32[]{:S(2)}, u32[]{:S(2)}) async-start(bf16[128,256,256]{2,1,0:T(8,128)(2,1)} %scatter_fusion.1), calls=%async_computation.1 | async-start | bytes 33554432 | tf_op jit(solution)/shard_map/all_to_all | solution.py:97
  293.8 0.1 copy.29
  293.9 1.7 fusion.25
  295.9 363.0 %all-to-all-done.1 = bf16[128,256,256]{2,1,0:T(8,128)(2,1)} async-done(((bf16[128,256,256]{2,1,0:T(8,128)(2,1)}), bf16[128,256,256]{2,1,0:T(8,128)(2,1)}, u32[]{:S(2)}, u32[]{:S(2)}) %all-to-all-start.1) | async-done | bytes 16777248 | tf_op jit(solution)/shard_map/all_to_all | solution.py:97
  658.8 0.1 broadcast_in_dim.19
  659.0 234.6 %while.23 = (s32[]{:T(128)}, f32[512,512]{1,0:T(8,128)S(1)}, s32[4,32]{1,0:T(4,128)S(1)}, bf16[4,32,256,256]{3,2,1,0:T(8,128)(2,1)}, s32[4,32]{1,0:T(4,128)S(1)}, /*index=5*/s32[]{:T(128)}) while((s32[]{:T(128)}, f32[512,512]{1,0:T(8,128)S(1)}, s32[4,32]{1,0:T(4,128)S(1)}, bf16[4,32,256,256]{3,2,1,0:T(8,128)(2,1)}, ...), condition=%wide.region_8.9_spmd.clone.clone, body=%wide.region_6.8_spmd.clone.clone.sunk | while | flops 2155913216 | bytes 71566664 | solution.py:119
  659.3 8.8 fusion.70
  668.3 49.5 %scatter_fusion = f32[512,512]{1,0:T(8,128)S(1)} fusion(f32[512,512]{1,0:T(8,128)S(1)} %get-tuple-element.267, s32[8192]{0:T(1024)S(1)} %bitcast.105, f32[8192,512]{1,0:T(8,128)} %bitcast.99), kind=kCustom, calls=%fused_computation.clone.clone.1 | custom fusion | flops 4194304 | bytes 50364416 | tf_op jit(solution)/shard_map/while/body/eval_jaxpr/scatter-add | solution.py:116
  717.9 8.8 fusion.70
  726.9 49.5 %scatter_fusion = f32[512,512]{1,0:T(8,128)S(1)} fusion(f32[512,512]{1,0:T(8,128)S(1)} %get-tuple-element.267, s32[8192]{0:T(1024)S(1)} %bitcast.105, f32[8192,512]{1,0:T(8,128)} %bitcast.99), kind=kCustom, calls=%fused_computation.clone.clone.1 | custom fusion | flops 4194304 | bytes 50364416 | tf_op jit(solution)/shard_map/while/body/eval_jaxpr/scatter-add | solution.py:116
  776.5 8.8 fusion.70
  785.5 49.5 %scatter_fusion = f32[512,512]{1,0:T(8,128)S(1)} fusion(f32[512,512]{1,0:T(8,128)S(1)} %get-tuple-element.267, s32[8192]{0:T(1024)S(1)} %bitcast.105, f32[8192,512]{1,0:T(8,128)} %bitcast.99), kind=kCustom, calls=%fused_computation.clone.clone.1 | custom fusion | flops 4194304 | bytes 50364416 | tf_op jit(solution)/shard_map/while/body/eval_jaxpr/scatter-add | solution.py:116
  835.0 8.8 fusion.70
  844.0 49.5 %scatter_fusion = f32[512,512]{1,0:T(8,128)S(1)} fusion(f32[512,512]{1,0:T(8,128)S(1)} %get-tuple-element.267, s32[8192]{0:T(1024)S(1)} %bitcast.105, f32[8192,512]{1,0:T(8,128)} %bitcast.99), kind=kCustom, calls=%fused_computation.clone.clone.1 | custom fusion | flops 4194304 | bytes 50364416 | tf_op jit(solution)/shard_map/while/body/eval_jaxpr/scatter-add | solution.py:116
  893.5 1.0 copy-done
  894.6 22.5 %reduce-scatter.3.cloned.1.call-done = f32[128,512]{1,0:T(8,128)} async-done(((f32[512,512]{1,0:T(8,128)}), f32[128,512]{1,0:T(8,128)}) %reduce-scatter.3.cloned.1.call-update) | async-done | bytes 262160 | tf_op jit(solution)/shard_map/reduce_scatter | solution.py:130
  917.0 1.8 divide_bitcast_fusion
  (59 shorter events, 2.1 us)
Async XLA Ops:
  90.9 193.3 %all-to-all-start = ((bf16[64,2,3]{2,1,0:T(2,128)(2,1)}), bf16[64,2,3]{2,1,0:T(2,128)(2,1)S(1)}, u32[]{:S(2)}, u32[]{:S(2)}) async-start(bf16[64,2,3]{2,1,0:T(2,128)(2,1)} %bitcast.10), calls=%async_computation | async-start | bytes 65536 | tf_op jit(solution)/shard_map/all_to_all | solution.py:98
  145.5 17.0 %copy-start.1 = (bf16[2,10]{1,0:T(2,128)(2,1)S(1)}, bf16[2,10]{1,0:T(2,128)(2,1)}, u32[]{:S(2)}) copy-start(bf16[2,10]{1,0:T(2,128)(2,1)} %param.16) | copy-start | bytes 124
  145.5 106.8 %copy-start.2 = (s32[4]{0:T(128)S(1)}, s32[4]{0:T(128)}, u32[]{:S(2)}) copy-start(s32[4]{0:T(128)} %param.13) | copy-start | bytes 52
  284.2 374.7 %all-to-all-start.1 = ((bf16[128,256,256]{2,1,0:T(8,128)(2,1)}), bf16[128,256,256]{2,1,0:T(8,128)(2,1)}, u32[]{:S(2)}, u32[]{:S(2)}) async-start(bf16[128,256,256]{2,1,0:T(8,128)(2,1)} %scatter_fusion.1), calls=%async_computation.1 | async-start | bytes 33554432 | tf_op jit(solution)/shard_map/all_to_all | solution.py:97
  293.5 601.1 %reduce-scatter.5.cloned.1.call-start = ((), (), s32[]{:S(2)}) async-start(), calls=%async_computation.5 | async-start | bytes 1310720 | tf_op jit(solution)/shard_map/reduce_scatter | solution.py:131
  295.7 621.4 %reduce-scatter.3.cloned.1.call-start = ((), (), s32[]{:S(2)}) async-start(), calls=%async_computation.4 | async-start | bytes 1310720 | tf_op jit(solution)/shard_map/reduce_scatter | solution.py:130
  893.5 1.0 copy-start
Sparse Core Ops, SparseCore 0:
  296.8 26.3 reduce-scatter.4
  894.7 22.3 reduce-scatter.2
where the time goes:
time: 930 us; the launch traced here: 926 us
  waiting for transfers between devices  385 us (41%)
  other arithmetic  202 us (22%)
  blocking collectives  168 us (18%)
  local copies, waits for them, and re-layouts  86.4 us (9%)
  matrix products  51.4 us (6%)
  starting transfers between devices  17.6 us (2%)
  between operations  13.6 us (1%)
    all_to_all x1, waiting for transfers between devices, per_device(): lax.all_to_all(send_tiles, 'exp', split_axis=0, concat_axis=0, tiled=True)  363 us
    scatter-add x4, other arithmetic, place_block(): canvas = canvas.at[row_index].add(shifted.reshape(-1, PS))  198 us
    all_gather x1, blocking collectives, per_device(): lax.all_gather(coeffs, ('exp', 'grp'), axis=0, tiled=True)  89.8 us
    unnamed x1, blocking collectives  78.6 us
    dot_general x4, matrix products, place_block(): jnp.einsum('syk,skx->syx', block_tiles, shifter, preferred_element_type=j...  35.3 us
    rev x2, local copies, waits for them, and re-layouts, band_matrix(): return window[:, ::-1, :].astype(jnp.bfloat16)  35.2 us
    reduce_scatter x1, waiting for transfers between devices, per_device(): lax.psum_scatter(flux, 'grp', scatter_dimension=0, tiled=True)  22.5 us
  transfers between devices with their start and end apart: 4, of which 2 were waited for; matrix products, arithmetic and copies ran while one was open for 36% of the time, Pallas kernels for 0%

commit v1 on v0

--- a/solution.py
+++ b/solution.py
@@ -51,8 +51,14 @@
     entries = tile_count * listed
     capacity = max(2, (entries + n_owners - 1) // n_owners)
     slot_total = n_owners * capacity
+    enter_desk_for = lambda local_values, across, row_dim: jnp.concatenate(
+        lax.all_to_all(
+            jnp.stack([local_values for _ in range(lax.psum(1, across))], 0), across, 0, 0
+        ),
+        row_dim,
+    )
     coef_all, weight_all = (
-        lax.all_gather(coeffs, ("exp", "grp"), axis=0, tiled=True),
+        enter_desk_for(coeffs, ("exp", "grp"), 0),
         lax.all_gather(inv_var, ("exp", "grp"), axis=0, tiled=True),
     )
     exposures = coef_all.shape[0]

time: 930 us -> 855 us (0.919)
  blocking collectives: 168 us -> 77.4 us
  starting transfers between devices: 17.6 us -> 33.9 us
    all_gather x1 -> x0, blocking collectives: 89.8 us -> none  [per_device(): lax.all_gather(coeffs, ('exp', 'grp'), axis=0, tiled=True)]
    all_to_all x0 -> x1, starting transfers between devices: none -> 14.6 us  [per_device(): lax.all_to_all(jnp.stack([local_values for _ in range(lax.psum(1, across)...]
  transfers between devices with their start and end apart: 4 -> 5, of which waited for: 2 -> 2; matrix products, arithmetic and copies ran while one was open for 36% -> 40% of each run, Pallas kernels for 0% -> 0%
where the time goes in v1:
time: 855 us; the launch traced here: 851 us
  waiting for transfers between devices  384 us (45%)
  other arithmetic  202 us (24%)
  local copies, waits for them, and re-layouts  87.4 us (10%)
  blocking collectives  77.4 us (9%)
  matrix products  51.3 us (6%)
  starting transfers between devices  33.9 us (4%)
  between operations  13.6 us (2%)
    all_to_all x1, waiting for transfers between devices, per_device(): lax.all_to_all(send_tiles, 'exp', split_axis=0, concat_axis=0, tiled=True)  363 us
    scatter-add x4, other arithmetic, place_block(): canvas = canvas.at[row_index].add(shifted.reshape(-1, PS))  198 us
    unnamed x1, blocking collectives  77.4 us
    dot_general x4, matrix products, place_block(): jnp.einsum('syk,skx->syx', block_tiles, shifter, preferred_element_type=j...  35.3 us
    rev x2, local copies, waits for them, and re-layouts, band_matrix(): return window[:, ::-1, :].astype(jnp.bfloat16)  35.2 us
    reduce_scatter x1, waiting for transfers between devices, per_device(): lax.psum_scatter(flux, 'grp', scatter_dimension=0, tiled=True)  21.4 us
  transfers between devices with their start and end apart: 5, of which 2 were waited for; matrix products, arithmetic and copies ran while one was open for 40% of the time, Pallas kernels for 0%

profile of v1, /device:TPU:8, one launch (start us, length us, event | category | flops | bytes accessed | tf_op | source)
XLA Modules:
  0.0 850.7 jit_solution(4699662942953374087)
XLA Ops:
  6.5 1.4 stack.6
  7.9 14.6 %all-to-all-start.1 = ((bf16[256,2,10]{2,1,0:T(2,128)(2,1)}), bf16[256,2,10]{2,1,0:T(2,128)(2,1)S(1)}, u32[]{:S(2)}, u32[]{:S(2)}) async-start(bf16[256,2,10]{2,1,0:T(2,128)(2,1)} %stack.6), calls=%async_computation.1 | async-start | bytes 262144 | tf_op jit(solution)/shard_map/all_to_all | solution.py:55
  22.5 0.8 eq.20
  23.3 0.7 broadcast_multiply_fusion
  24.1 0.2 select_reduce_fusion
  24.4 0.8 dynamic-update-slice
  25.2 77.4 %all-reduce = bf16[512]{0:T(512)(128)(2,1)S(1)} all-reduce(bf16[512]{0:T(512)(128)(2,1)S(1)} %dynamic-update-slice), channel_id=1, replica_groups=mesh['exp'=64,'grp'=4] {'exp','grp'}, use_global_device_ids=true, to_apply=%add | all-reduce | flops 512 | bytes 2048
  102.6 0.8 fusion.48
  103.6 0.7 copy.16
  104.5 0.8 maximum_maximum_fusion.1
  105.3 0.1 copy.17
  105.4 0.2 tile.8
  105.6 0.3 pad.9
  105.9 1.6 copy.31
  107.4 2.1 slice.39
  109.5 8.3 reshape.151
  117.9 1.2 slice.40
  119.0 19.4 %rev.6 = bf16[10,256,256]{2,1,0:T(8,128)(2,1)} reverse(bf16[10,256,256]{2,1,0:T(8,128)(2,1)} %slice.40), dimensions={1} | reverse | bytes 2621440 | tf_op jit(solution)/shard_map/rev | solution.py:24
  138.4 0.2 tile.20
  138.6 0.3 pad.10
  138.9 1.6 copy.32
  140.4 2.1 slice.41
  142.5 8.3 reshape.153
  150.9 1.2 slice.42
  152.1 15.8 %rev.7 = bf16[10,256,256]{2,1,0:T(8,128)(2,1)S(1)} reverse(bf16[10,256,256]{2,1,0:T(8,128)(2,1)} %slice.42), dimensions={1} | reverse | bytes 2621440 | tf_op jit(solution)/shard_map/rev | solution.py:24
  167.9 1.2 scatter_custom_fusion.1
  169.1 8.8 %all-to-all-start = ((bf16[64,2,3]{2,1,0:T(2,128)(2,1)}), bf16[64,2,3]{2,1,0:T(2,128)(2,1)S(1)}, u32[]{:S(2)}, u32[]{:S(2)}) async-start(bf16[64,2,3]{2,1,0:T(2,128)(2,1)} %bitcast.10), calls=%async_computation | async-start | bytes 65536 | tf_op jit(solution)/shard_map/all_to_all | solution.py:104
  177.8 0.2 fusion.39
  178.0 18.7 %while.22 = (s32[]{:T(128)}, bf16[4,256,256]{2,1,0:T(8,128)(2,1)}, f32[4]{0:T(128)S(1)}, bf16[4,256,256]{2,1,0:T(8,128)(2,1)}, bf16[10,256,256]{2,1,0:T(8,128)(2...) while((s32[]{:T(128)}, bf16[4,256,256]{2,1,0:T(8,128)(2,1)}, f32[4]{0:T(128)S(1)}, ...), condition=%wide.region_3.4_spmd, body=%wide.region_2.3_spmd.sunk | while | flops 672530432 | bytes 3409629 | solution.py:82
  178.0 0.6 dynamic_slice.54
  178.6 3.3 fusion.66
  181.9 0.1 copy.35
  182.0 0.7 constant_dynamic-update-slice_fusion.2
  182.7 0.6 dynamic_slice.54
  183.3 3.3 fusion.66
  186.6 0.1 copy.35
  186.8 0.7 constant_dynamic-update-slice_fusion.2
  187.4 0.6 dynamic_slice.54
  188.0 3.3 fusion.66
  191.3 0.1 copy.35
  191.4 0.7 constant_dynamic-update-slice_fusion.2
  192.1 0.6 dynamic_slice.54
  192.7 3.3 fusion.66
  196.0 0.1 copy.35
  196.1 0.7 constant_dynamic-update-slice_fusion.2
  196.8 1.2 broadcast_in_dim.30
  198.0 5.9 broadcast_in_dim.28
  204.0 5.3 scatter_fusion.1
  209.2 10.4 %all-to-all-start.2 = ((bf16[128,256,256]{2,1,0:T(8,128)(2,1)}), bf16[128,256,256]{2,1,0:T(8,128)(2,1)}, u32[]{:S(2)}, u32[]{:S(2)}) async-start(bf16[128,256,256]{2,1,0:T(8,128)(2,1)} %scatter_fusion.1), calls=%async_computation.2 | async-start | bytes 33554432 | tf_op jit(solution)/shard_map/all_to_all | solution.py:103
  220.1 1.7 fusion.25
  222.1 363.0 %all-to-all-done.2 = bf16[128,256,256]{2,1,0:T(8,128)(2,1)} async-done(((bf16[128,256,256]{2,1,0:T(8,128)(2,1)}), bf16[128,256,256]{2,1,0:T(8,128)(2,1)}, u32[]{:S(2)}, u32[]{:S(2)}) %all-to-all-start.2) | async-done | bytes 16777248 | tf_op jit(solution)/shard_map/all_to_all | solution.py:103
  585.0 0.1 broadcast_in_dim.19
  585.2 234.5 %while.23 = (s32[]{:T(128)}, f32[512,512]{1,0:T(8,128)S(1)}, s32[4,32]{1,0:T(4,128)S(1)}, bf16[4,32,256,256]{3,2,1,0:T(8,128)(2,1)}, s32[4,32]{1,0:T(4,128)S(1)}, /*index=5*/s32[]{:T(128)}) while((s32[]{:T(128)}, f32[512,512]{1,0:T(8,128)S(1)}, s32[4,32]{1,0:T(4,128)S(1)}, bf16[4,32,256,256]{3,2,1,0:T(8,128)(2,1)}, ...), condition=%wide.region_8.9_spmd.clone.clone, body=%wide.region_6.8_spmd.clone.clone.sunk | while | flops 2155913216 | bytes 71566664 | solution.py:125
  585.5 8.8 %fusion.70 = f32[32,256,512]{2,1,0:T(8,128)} fusion(s32[32,256]{1,0:T(8,128)S(1)} %iota_add_fusion.3, bf16[4,32,256,256]{3,2,1,0:T(8,128)(2,1)} %get-tuple-element.275, s32[]{:T(128)} %get-tuple-element.266), kind=kOutput, calls=%fused_computation.19.clone.1 | convolution fusion | flops 2151677952 | bytes 21004800 | tf_op jit(solution)/shard_map/while/body/eval_jaxpr/syk,skx->syx/dot_general | solution.py:118
  594.5 49.5 %scatter_fusion = f32[512,512]{1,0:T(8,128)S(1)} fusion(f32[512,512]{1,0:T(8,128)S(1)} %get-tuple-element.267, s32[8192]{0:T(1024)S(1)} %bitcast.104, f32[8192,512]{1,0:T(8,128)} %bitcast.98), kind=kCustom, calls=%fused_computation.clone.clone.1 | custom fusion | flops 4194304 | bytes 50364416 | tf_op jit(solution)/shard_map/while/body/eval_jaxpr/scatter-add | solution.py:122
  644.1 8.8 %fusion.70 = f32[32,256,512]{2,1,0:T(8,128)} fusion(s32[32,256]{1,0:T(8,128)S(1)} %iota_add_fusion.3, bf16[4,32,256,256]{3,2,1,0:T(8,128)(2,1)} %get-tuple-element.275, s32[]{:T(128)} %get-tuple-element.266), kind=kOutput, calls=%fused_computation.19.clone.1 | convolution fusion | flops 2151677952 | bytes 21004800 | tf_op jit(solution)/shard_map/while/body/eval_jaxpr/syk,skx->syx/dot_general | solution.py:118
  653.0 49.5 %scatter_fusion = f32[512,512]{1,0:T(8,128)S(1)} fusion(f32[512,512]{1,0:T(8,128)S(1)} %get-tuple-element.267, s32[8192]{0:T(1024)S(1)} %bitcast.104, f32[8192,512]{1,0:T(8,128)} %bitcast.98), kind=kCustom, calls=%fused_computation.clone.clone.1 | custom fusion | flops 4194304 | bytes 50364416 | tf_op jit(solution)/shard_map/while/body/eval_jaxpr/scatter-add | solution.py:122
  702.6 8.8 %fusion.70 = f32[32,256,512]{2,1,0:T(8,128)} fusion(s32[32,256]{1,0:T(8,128)S(1)} %iota_add_fusion.3, bf16[4,32,256,256]{3,2,1,0:T(8,128)(2,1)} %get-tuple-element.275, s32[]{:T(128)} %get-tuple-element.266), kind=kOutput, calls=%fused_computation.19.clone.1 | convolution fusion | flops 2151677952 | bytes 21004800 | tf_op jit(solution)/shard_map/while/body/eval_jaxpr/syk,skx->syx/dot_general | solution.py:118
  711.6 49.5 %scatter_fusion = f32[512,512]{1,0:T(8,128)S(1)} fusion(f32[512,512]{1,0:T(8,128)S(1)} %get-tuple-element.267, s32[8192]{0:T(1024)S(1)} %bitcast.104, f32[8192,512]{1,0:T(8,128)} %bitcast.98), kind=kCustom, calls=%fused_computation.clone.clone.1 | custom fusion | flops 4194304 | bytes 50364416 | tf_op jit(solution)/shard_map/while/body/eval_jaxpr/scatter-add | solution.py:122
  761.2 8.8 %fusion.70 = f32[32,256,512]{2,1,0:T(8,128)} fusion(s32[32,256]{1,0:T(8,128)S(1)} %iota_add_fusion.3, bf16[4,32,256,256]{3,2,1,0:T(8,128)(2,1)} %get-tuple-element.275, s32[]{:T(128)} %get-tuple-element.266), kind=kOutput, calls=%fused_computation.19.clone.1 | convolution fusion | flops 2151677952 | bytes 21004800 | tf_op jit(solution)/shard_map/while/body/eval_jaxpr/syk,skx->syx/dot_general | solution.py:118
  770.2 49.5 %scatter_fusion = f32[512,512]{1,0:T(8,128)S(1)} fusion(f32[512,512]{1,0:T(8,128)S(1)} %get-tuple-element.267, s32[8192]{0:T(1024)S(1)} %bitcast.104, f32[8192,512]{1,0:T(8,128)} %bitcast.98), kind=kCustom, calls=%fused_computation.clone.clone.1 | custom fusion | flops 4194304 | bytes 50364416 | tf_op jit(solution)/shard_map/while/body/eval_jaxpr/scatter-add | solution.py:122
  819.7 1.0 copy-done
  820.7 21.4 %reduce-scatter.3.cloned.1.call-done = f32[128,512]{1,0:T(8,128)} async-done(((f32[512,512]{1,0:T(8,128)}), f32[128,512]{1,0:T(8,128)}) %reduce-scatter.3.cloned.1.call-update) | async-done | bytes 262160 | tf_op jit(solution)/shard_map/reduce_scatter | solution.py:136
  842.1 1.8 divide_bitcast_fusion
  (59 shorter events, 2.2 us)
Async XLA Ops:
  7.9 161.1 %all-to-all-start.1 = ((bf16[256,2,10]{2,1,0:T(2,128)(2,1)}), bf16[256,2,10]{2,1,0:T(2,128)(2,1)S(1)}, u32[]{:S(2)}, u32[]{:S(2)}) async-start(bf16[256,2,10]{2,1,0:T(2,128)(2,1)} %stack.6), calls=%async_computation.1 | async-start | bytes 262144 | tf_op jit(solution)/shard_map/all_to_all | solution.py:55
  150.9 27.0 %copy-start.1 = (s32[4]{0:T(128)S(1)}, s32[4]{0:T(128)}, u32[]{:S(2)}) copy-start(s32[4]{0:T(128)} %param.13) | copy-start | bytes 52
  169.1 40.2 %all-to-all-start = ((bf16[64,2,3]{2,1,0:T(2,128)(2,1)}), bf16[64,2,3]{2,1,0:T(2,128)(2,1)S(1)}, u32[]{:S(2)}, u32[]{:S(2)}) async-start(bf16[64,2,3]{2,1,0:T(2,128)(2,1)} %bitcast.10), calls=%async_computation | async-start | bytes 65536 | tf_op jit(solution)/shard_map/all_to_all | solution.py:104
  209.2 375.8 %all-to-all-start.2 = ((bf16[128,256,256]{2,1,0:T(8,128)(2,1)}), bf16[128,256,256]{2,1,0:T(8,128)(2,1)}, u32[]{:S(2)}, u32[]{:S(2)}) async-start(bf16[128,256,256]{2,1,0:T(8,128)(2,1)} %scatter_fusion.1), calls=%async_computation.2 | async-start | bytes 33554432 | tf_op jit(solution)/shard_map/all_to_all | solution.py:103
  219.7 601.1 %reduce-scatter.5.cloned.1.call-start = ((), (), s32[]{:S(2)}) async-start(), calls=%async_computation.6 | async-start | bytes 1310720 | tf_op jit(solution)/shard_map/reduce_scatter | solution.py:137
  221.9 620.2 %reduce-scatter.3.cloned.1.call-start = ((), (), s32[]{:S(2)}) async-start(), calls=%async_computation.5 | async-start | bytes 1310720 | tf_op jit(solution)/shard_map/reduce_scatter | solution.py:136
  819.7 1.0 copy-start
Sparse Core Ops, SparseCore 0:
  223.0 25.2 reduce-scatter.4
  820.8 21.2 reduce-scatter.2
